TPU v7x, 256 devices: a whole 4x4x8 slice. The times are simulated.
256 devices in a mesh: circ: 8 (over y_lo, x), span: 32 (over y_hi, z, core).
Axes of the slice: x: 4, y: 4 (y_hi: 2, y_lo: 2; y = y_hi * 2 + y_lo), z: 8, core: 2. Of those that a mesh axis runs over, the one named last changes fastest.
Arguments:
- q_old: float32 [5, 32, 4096, 128], P(None, 'circ', 'span'), may hold values from -6 to 6
- pseudo_rate: float32 [32, 4096, 128], P('circ', 'span'), may hold values from 0.15 to 0.45
- flux_jacobians: float32 [3, 5, 5], replicated, may hold values from -2.5 to 2.5
- rotor_face: float32 [5, 32, 4096], P(None, 'circ', 'span'), may hold values from -6 to 6
- offsets: int32 [4096], P('span'), may hold values from 0 to 31
- owners: int32 [8, 128, 4], P('circ', 'span'), may hold values from 0 to 31, all different within a row; in each aligned block of 4 rows (0 to 3, 4 to 7, ..., all dimensions but the last counted through in order) at most 2 rows name the same one
- slots: int32 [8, 128, 4], P('circ', 'span'), may hold values from 0 to 3
- weight_idx: int32 [8, 128, 4], P('circ', 'span'), may hold values from 0 to 15
- weight_table: float32 [16], replicated, may hold values from 0.3 to 1
Outputs:
- q_new: float32 [5, 32, 4096, 128], P(None, 'circ', 'span')
Inputs may be any that keep to these rules, and one draw needn't show every extreme that they name: The 4 owners of one rotor panel differ; among the 4 rotor panels of one device in one circumferential block, no owner is named more than 2 times, and that count is reached.
All inputs are finite; a program needn't handle non-finite values.
Results may differ from a plain program's by a relative error of at most 0.000068.
Values sent between devices are 32-bit elements; how exact they have to be, the bound alone decides.
No kernel may reach another device: no remote copies, remote signals or barrier semaphores. Data moves between devices by JAX's collectives and lax.ppermute only.
A program may use at most 64 MiB of HBM per device.

v0:
```python
import jax
import jax.numpy as jnp
from jax import lax
from jax.sharding import PartitionSpec as P

NF = 5
KP_DEV = 4
PW = 32
inv_step = 0.5
viscosity = 0.1


def with_halo(block, sides, width):
    for axis, dim in sides:
        count = lax.axis_size(axis)
        forward = [(i, i + 1) for i in range(count - 1)]
        forward.append((count - 1, 0))
        backward = [(target, source) for source, target in forward]
        low = lax.ppermute(
            lax.slice_in_dim(block, block.shape[dim] - width, None, axis=dim), axis, forward
        )
        high = lax.ppermute(lax.slice_in_dim(block, 0, width, axis=dim), axis, backward)
        block = jnp.concatenate([low, block, high], axis=dim)
    return block


def contract(matrix, values):
    return jnp.einsum("fg,gtsa->ftsa", matrix, values, precision=lax.Precision.HIGHEST)


def advance(padded, current, previous, rate_cells, inlet_plane, jacobians):
    circ_up = padded[:, 2:, 1:-1]
    circ_down = padded[:, :-2, 1:-1]
    span_up = padded[:, 1:-1, 2:]
    span_down = padded[:, 1:-1, :-2]
    zero_column = jnp.zeros_like(current[..., :1])
    axial_up = jnp.concatenate([current[..., 1:], zero_column], axis=-1)
    axial_down = jnp.concatenate([inlet_plane[..., None], current[..., :-1]], axis=-1)
    convection = contract(jacobians[0], circ_up - circ_down)
    convection = convection + contract(jacobians[1], span_up - span_down)
    convection = convection + contract(jacobians[2], axial_up - axial_down)
    laplacian = (
        circ_up + circ_down + (span_up + span_down) + (axial_up + axial_down) - 6.0 * current
    )
    residual = inv_step * (current - previous) + 0.5 * convection - viscosity * laplacian
    return current - rate_cells[None] * residual


def wall_zero(field_array, width):
    span_index = lax.axis_index("span")
    span_count = lax.axis_size("span")
    length = field_array.shape[2]
    position = jnp.arange(length, dtype=jnp.int32)
    at_hub = jnp.logical_and(span_index == 0, position < width)
    at_tip = jnp.logical_and(span_index == span_count - 1, position >= length - width)
    keeping = jnp.logical_not(jnp.logical_or(at_hub, at_tip)).astype(field_array.dtype)
    keeping = keeping.reshape(1, 1, length, 1)
    return field_array * keeping


def body(
    q_old, pseudo_rate, flux_jacobians, rotor_face, offsets, owners, slots, weight_idx, weight_table
):
    circ_count = lax.axis_size("circ")
    rows_local = rotor_face.shape[1]
    total_rows = rows_local * circ_count
    row_iota = jnp.arange(rows_local, dtype=jnp.int32)
    all_rows = lax.all_gather(rotor_face, "circ", axis=1, tiled=True)
    first_row = lax.axis_index("circ") * rows_local
    source_rows = (first_row + row_iota[:, None] - offsets[None, :]) % total_rows
    rotated = jnp.take_along_axis(all_rows, source_rows[None], axis=1)
    panels = rotated.reshape(NF, rows_local, KP_DEV, PW)
    table_ids = jnp.arange(weight_table.shape[0], dtype=jnp.int32)
    weights = jnp.sum(jnp.where(weight_idx[..., None] == table_ids, weight_table, 0.0), axis=-1)
    targets = owners[0] * KP_DEV + slots[0]
    local_weights = weights[0]
    panel_ids = jnp.arange(KP_DEV * lax.axis_size("span"), dtype=jnp.int32)
    mixing = jnp.sum(
        jnp.where(targets[None] == panel_ids[:, None, None], local_weights[None], 0.0), axis=-1
    )
    span_count = lax.axis_size("span")
    contributions = jnp.einsum("gk,ftkp->gftp", mixing, panels, precision=lax.Precision.HIGHEST)
    contributions = contributions.reshape((span_count, KP_DEV) + contributions.shape[1:])
    received = lax.all_to_all(contributions, "span", 0, 0, tiled=True)
    own_panels = jnp.sum(received, axis=0)
    inlet_plane = jnp.transpose(own_panels, (1, 2, 0, 3)).reshape(NF, rows_local, KP_DEV * PW)

    def sweep(current):
        padded = with_halo(current, (("circ", 1), ("span", 2)), 1)
        padded = wall_zero(padded, 1)
        return advance(padded, current, q_old, pseudo_rate, inlet_plane, flux_jacobians)

    first_pass = sweep(q_old)
    return sweep(first_pass)


def solution(mesh):
    return jax.shard_map(
        body,
        mesh=mesh,
        in_specs=(
            P(None, "circ", "span", None),
            P("circ", "span", None),
            P(),
            P(None, "circ", "span"),
            P("span"),
            P("circ", "span", None),
            P("circ", "span", None),
            P("circ", "span", None),
            P(),
        ),
        out_specs=P(None, "circ", "span", None),
        check_vma=False,
    )
```

profile of v0, /device:TPU:6, one launch (start us, length us, event | category | flops | bytes accessed | tf_op | source)
XLA Modules:
  0.0 128.1 jit_solution(10286612032993077256)
XLA Ops:
  0.0 1.2 fusion.49
  1.2 1.0 copy.118
  2.2 1.5 %collective-permute-start = (f32[5,1,128,128]{3,0,2,1:T(8,128)}, f32[5,1,128,128]{3,0,2,1:T(8,128)}, u32[]{:S(2)}, u32[]{:S(2)}) collective-permute-start(f32[5,1,128,128]{3,0,2,1:T(8,128)} %copy.118), channel_id=1, source_target_pairs={{0,32},{32,64},{64,96},{96,128},{128,160},{160,192},{192,224},{224... | collective-permute-start | bytes 983048 | tf_op jit(solution)/shard_map/ppermute | solution.py:19
  3.7 1.0 copy.119
  4.7 0.5 collective-permute-start.1
  5.3 0.1 compare_and_fusion
  5.3 0.1 fusion.41
  5.5 0.0 copy-done.11
  5.5 0.0 copy-done.10
  5.5 0.2 select_reduce_fusion.1
  5.7 0.1 select_reduce_fusion
  5.7 0.1 dot_general.25
  5.9 0.1 copy.93
  6.0 36.6 %all_gather.3 = f32[5,32,128]{2,0,1:T(8,128)S(1)} all-gather(f32[5,4,128]{2,0,1:T(8,128)S(1)} %copy.76), channel_id=1, replica_groups=mesh['circ'=8,'span'=32] {'circ'}, dimensions={1}, use_global_device_ids=true | all-gather | bytes 92160 | tf_op jit(solution)/shard_map/all_gather | solution.py:68
  42.5 0.6 copy.77
  43.2 3.5 %gather_fusion = f32[512,5]{1,0:T(8,128)S(1)} fusion(f32[5,32,128]{0,2,1:T(8,128)S(1)} %copy.77, s32[512]{0:T(512)S(1)} %fusion.41), kind=kCustom, calls=%fused_computation | custom fusion | bytes 24576 | tf_op jit(solution)/shard_map/jit(take_along_axis)/gather | solution.py:71
  46.7 0.1 broadcast_select_fusion
  46.8 0.2 copy.97
  47.0 1.3 fusion.34
  48.3 0.0 copy-start.7
  48.3 0.0 copy-start
  48.3 0.8 copy.80
  49.2 1.6 %reshape.183 = f32[32,1,2560]{2,1,0:T(1,128)} reshape(f32[32,4,5,4,32]{4,3,2,1,0:T(4,128)S(1)} %copy.80) | data formatting | bytes 655360
  50.7 11.2 %all-to-all-start = ((f32[32,1,2560]{2,1,0:T(1,128)}), f32[32,1,2560]{2,1,0:T(1,128)S(1)}, u32[]{:S(2)}, u32[]{:S(2)}) async-start(f32[32,1,2560]{2,1,0:T(1,128)} %reshape.183), calls=%async_computation | async-start | bytes 655360 | tf_op jit(solution)/shard_map/all_to_all | solution.py:84
  62.0 0.4 fusion.50
  62.4 0.0 collective-permute-done
  62.4 1.1 constant_dynamic-update-slice_fusion.1
  63.5 0.8 copy_dynamic-update-slice_fusion
  64.3 0.0 collective-permute-done.1
  64.4 1.1 constant_dynamic-update-slice_fusion
  65.4 0.4 collective-permute-start.2
  65.8 5.2 %collective-permute-start.3 = (f32[5,6,1,128]{3,0,2,1:T(8,128)S(1)}, f32[5,6,1,128]{3,0,2,1:T(8,128)S(1)}, u32[]{:S(2)}, u32[]{:S(2)}) collective-permute-start(f32[5,6,1,128]{3,0,2,1:T(8,128)S(1)} %get-tuple-element.8), channel_id=1, source_target_pairs={{1,0},{2,1},{3,2},{4,3},{5,4},{6,5},{7,6},{8,7},{9,8},{10,9},{11,1... | collective-permute-start | bytes 46088 | tf_op jit(solution)/shard_map/ppermute | solution.py:22
  71.0 2.2 %copy.117 = f32[5,4,128,127]{3,0,2,1:T(8,128)} copy(f32[5,4,128,127]{3,2,1,0:T(8,128)S(1)} %get-tuple-element.15) | data formatting | bytes 2600960
  73.2 2.2 %copy.116 = f32[5,4,128,127]{3,0,2,1:T(8,128)} copy(f32[5,4,128,127]{3,2,1,0:T(8,128)S(1)} %get-tuple-element.16) | data formatting | bytes 2600960
  75.4 0.0 collective-permute-done.2
  75.4 0.0 collective-permute-done.3
  75.4 0.3 maximum_multiply_fusion
  75.7 1.7 %copy-done.3 = f32[5,6,130,128]{3,0,2,1:T(8,128)} copy-done((f32[5,6,130,128]{3,0,2,1:T(8,128)}, f32[5,6,130,128]{3,0,2,1:T(8,128)S(1)}, u32[]{:S(2)}) %copy-start.3) | copy-done | bytes 1996824
  77.4 3.4 %fusion.20 = f32[4,128,128,5]{2,3,1,0:T(8,128)} fusion(f32[5,6,130,128]{3,0,2,1:T(8,128)S(1)} %maximum_multiply_fusion, f32[1,5,5]{2,0,1:T(1,128)S(1)} %get-tuple-element.18), kind=kOutput, calls=%fused_computation.25 | convolution fusion | flops 19988480 | bytes 5507584 | tf_op jit(solution)/shard_map/fg,gtsa->ftsa/dot_general | solution.py:28
  80.8 0.0 all-to-all-done
  80.8 0.5 broadcast.283
  81.3 1.4 %reduce.1 = f32[32,2560]{1,0:T(8,128)S(1)} reduce(f32[32,1,2560]{2,1,0:T(1,128)S(1)} %all-to-all-done, f32[]{:T(128)} %broadcast.283), dimensions={1}, to_apply=%all_to_all.3.reduce_sub_computation | reduce | bytes 655364 | tf_op jit(solution)/shard_map/all_to_all | solution.py:84
  82.7 0.7 reshape.184
  83.4 0.3 reduce_sum.29
  83.7 0.9 copy.98
  84.5 1.4 %reshape.182 = f32[5,4,128,1]{3,0,2,1:T(8,128)S(1)} reshape(f32[5,4,4,32]{0,3,2,1:T(8,128)} %copy.98) | data formatting | bytes 20480 | tf_op jit(solution)/shard_map/broadcast_in_dim;reshape | solution.py:38
  86.0 0.0 copy-start.5
  86.0 4.9 %fusion.18 = f32[4,128,128,5]{2,3,1,0:T(8,128)S(1)} fusion(f32[5,4,128,127]{3,0,2,1:T(8,128)} %copy.116, f32[5,4,128,127]{3,0,2,1:T(8,128)} %copy.117, f32[5,4,128,1]{3,0,2,1:T(8,128)S(1)} %reshape.182, f32[1,5,5]{2,0,1:T(1,128)S(1)} %get-tuple-element.19), kind=kOutput, calls=%fused_computation.23 | convolution fusion | flops 20316160 | bytes 3922020 | tf_op jit(solution)/shard_map/fg,gtsa->ftsa/dot_general | solution.py:28
  90.9 7.1 %fusion.7 = f32[5,4,128,128]{3,0,2,1:T(8,128)S(1)} fusion(f32[4,128,128,5]{2,3,1,0:T(8,128)S(1)} %fusion.18, f32[4,128,128,5]{2,3,1,0:T(8,128)} %fusion.20, f32[5,6,130,128]{3,0,2,1:T(8,128)S(1)} %copy-done.4, f32[5,4,128,127]{3,0,2,1:T(8,128)S(1)} %copy-done.2, f32[4,128,128]{2,1,0:T(8,128)S(1)} %copy-done.5, f32[5,4,128,128]{3,2,1,0:T(8,128)S(1)} %copy-done, ...), kind=kOutput, calls=%fused_computation.14 | convolution fusion | flops 25559040 | bytes 25168384 | tf_op jit(solution)/shard_map/fg,gtsa->ftsa/dot_general | solution.py:28
  98.0 0.1 fusion.47
  98.1 0.1 collective-permute-start.4
  98.2 2.0 %collective-permute-start.5 = (f32[5,1,128,128]{3,0,2,1:T(8,128)S(1)}, f32[5,1,128,128]{3,0,2,1:T(8,128)S(1)}, u32[]{:S(2)}, u32[]{:S(2)}) collective-permute-start(f32[5,1,128,128]{3,0,2,1:T(8,128)S(1)} %get-tuple-element.10), channel_id=1, source_target_pairs={{32,0},{64,32},{96,64},{128,96},{160,128},{192,160},{224,192},{0,2... | collective-permute-start | bytes 983048 | tf_op jit(solution)/shard_map/ppermute | solution.py:22
  100.2 0.7 fusion.48
  100.9 7.9 %collective-permute-done.4 = f32[5,1,128,128]{3,0,2,1:T(8,128)S(1)} collective-permute-done((f32[5,1,128,128]{3,0,2,1:T(8,128)S(1)}, f32[5,1,128,128]{3,0,2,1:T(8,128)S(1)}, u32[]{:S(2)}, u32[]{:S(2)}) %collective-permute-start.4) | collective-permute-done | bytes 327712 | tf_op jit(solution)/shard_map/ppermute | solution.py:19
  108.8 2.4 %collective-permute-done.5 = f32[5,1,128,128]{3,0,2,1:T(8,128)S(1)} collective-permute-done((f32[5,1,128,128]{3,0,2,1:T(8,128)S(1)}, f32[5,1,128,128]{3,0,2,1:T(8,128)S(1)}, u32[]{:S(2)}, u32[]{:S(2)}) %collective-permute-start.5) | collective-permute-done | bytes 327712 | tf_op jit(solution)/shard_map/ppermute | solution.py:22
  111.2 0.1 collective-permute-start.6
  111.3 5.5 %collective-permute-start.7 = (f32[5,6,1,128]{3,0,2,1:T(8,128)S(1)}, f32[5,6,1,128]{3,0,2,1:T(8,128)S(1)}, u32[]{:S(2)}, u32[]{:S(2)}) collective-permute-start(f32[5,6,1,128]{3,0,2,1:T(8,128)S(1)} %get-tuple-element.6), channel_id=1, source_target_pairs={{1,0},{2,1},{3,2},{4,3},{5,4},{6,5},{7,6},{8,7},{9,8},{10,9},{11,1... | collective-permute-start | bytes 46088 | tf_op jit(solution)/shard_map/ppermute | solution.py:22
  116.8 2.5 %fusion.8 = f32[4,128,128,5]{2,3,1,0:T(8,128)S(1)} fusion(f32[5,4,128,127]{3,0,2,1:T(8,128)S(1)} %get-tuple-element.12, f32[5,4,128,127]{3,0,2,1:T(8,128)S(1)} %get-tuple-element.11, f32[5,4,128,1]{3,0,2,1:T(8,128)S(1)} %reshape.182, f32[1,5,5]{2,0,1:T(1,128)S(1)} %get-tuple-element.19), kind=kOutput, calls=%fused_computation.15 | convolution fusion | flops 20316160 | bytes 3922020 | tf_op jit(solution)/shard_map/fg,gtsa->ftsa/dot_general | solution.py:28
  119.3 0.0 collective-permute-done.6
  119.3 0.0 collective-permute-done.7
  119.3 0.4 maximum_multiply_fusion.1
  119.7 2.0 %fusion.10 = f32[4,128,128,5]{2,3,1,0:T(8,128)S(1)} fusion(f32[5,6,130,128]{3,0,2,1:T(8,128)S(1)} %maximum_multiply_fusion.1, f32[1,5,5]{2,0,1:T(1,128)S(1)} %get-tuple-element.18), kind=kOutput, calls=%fused_computation.17 | convolution fusion | flops 19988480 | bytes 5507584 | tf_op jit(solution)/shard_map/fg,gtsa->ftsa/dot_general | solution.py:28
  121.7 5.0 %fusion.3 = f32[5,4,128,128]{3,0,2,1:T(8,128)S(1)} fusion(f32[5,4,128,128]{3,0,2,1:T(8,128)S(1)} %fusion.7, f32[4,128,128,5]{2,3,1,0:T(8,128)S(1)} %fusion.8, f32[4,128,128,5]{2,3,1,0:T(8,128)S(1)} %fusion.10, f32[5,6,130,128]{3,0,2,1:T(8,128)S(1)} %maximum_multiply_fusion.1, f32[5,4,128,127]{3,0,2,1:T(8,128)S(1)} %get-tuple-element.12, ...), kind=kOutput, calls=%fused_computation.9 | convolution fusion | flops 25559040 | bytes 28051968 | tf_op jit(solution)/shard_map/fg,gtsa->ftsa/dot_general | solution.py:28
  126.8 1.3 %copy.90 = f32[5,4,128,128]{3,2,1,0:T(8,128)} copy(f32[5,4,128,128]{3,0,2,1:T(8,128)S(1)} %fusion.3) | data formatting | bytes 2621440 | tf_op jit(solution)/shard_map/sub | solution.py:46
  (27 shorter events, 0.1 us)
Async XLA Ops:
  0.0 5.3 %copy-start.12 = (s32[128]{0:T(128)S(1)}, s32[128]{0:T(128)}, u32[]{:S(2)}) copy-start(s32[128]{0:T(128)} %param.13) | copy-start | bytes 1540
  0.0 5.4 %copy-start.6 = (f32[5,4,128]{2,1,0:T(4,128)S(1)}, f32[5,4,128]{2,1,0:T(4,128)}, u32[]{:S(2)}) copy-start(f32[5,4,128]{2,1,0:T(4,128)} %param.12) | copy-start | bytes 30724
  0.0 5.4 %copy-start.8 = (s32[1,4,4]{2,1,0:T(4,128)S(1)}, s32[1,4,4]{2,1,0:T(4,128)}, u32[]{:S(2)}) copy-start(s32[1,4,4]{2,1,0:T(4,128)} %param.15) | copy-start | bytes 196
  0.0 5.4 %copy-start.9 = (s32[1,4,4]{2,1,0:T(4,128)S(1)}, s32[1,4,4]{2,1,0:T(4,128)}, u32[]{:S(2)}) copy-start(s32[1,4,4]{2,1,0:T(4,128)} %param.14) | copy-start | bytes 196
  0.0 5.5 %copy-start.11 = (f32[16]{0:T(128)S(1)}, f32[16]{0:T(128)}, u32[]{:S(2)}) copy-start(f32[16]{0:T(128)} %param.17) | copy-start | bytes 196
  0.0 5.5 %copy-start.10 = (s32[1,4,4]{2,1,0:T(4,128)S(1)}, s32[1,4,4]{2,1,0:T(4,128)}, u32[]{:S(2)}) copy-start(s32[1,4,4]{2,1,0:T(4,128)} %param.16) | copy-start | bytes 196
  2.2 60.2 %collective-permute-start = (f32[5,1,128,128]{3,0,2,1:T(8,128)}, f32[5,1,128,128]{3,0,2,1:T(8,128)}, u32[]{:S(2)}, u32[]{:S(2)}) collective-permute-start(f32[5,1,128,128]{3,0,2,1:T(8,128)} %copy.118), channel_id=1, source_target_pairs={{0,32},{32,64},{64,96},{96,128},{128,160},{160,192},{192,224},{224... | collective-permute-start | bytes 983048 | tf_op jit(solution)/shard_map/ppermute | solution.py:19
  4.7 59.6 %collective-permute-start.1 = (f32[5,1,128,128]{3,0,2,1:T(8,128)}, f32[5,1,128,128]{3,0,2,1:T(8,128)}, u32[]{:S(2)}, u32[]{:S(2)}) collective-permute-start(f32[5,1,128,128]{3,0,2,1:T(8,128)} %copy.119), channel_id=1, source_target_pairs={{32,0},{64,32},{96,64},{128,96},{160,128},{192,160},{224,192},{0,2... | collective-permute-start | bytes 983048 | tf_op jit(solution)/shard_map/ppermute | solution.py:22
  48.3 13.7 %copy-start.7 = (f32[3,5,5]{2,0,1:T(4,128)S(1)}, f32[3,5,5]{2,0,1:T(4,128)}, u32[]{:S(2)}) copy-start(f32[3,5,5]{2,0,1:T(4,128)} %param.11) | copy-start | bytes 904
  48.3 13.7 %copy-start = (f32[5,4,128,128]{3,2,1,0:T(8,128)S(1)}, f32[5,4,128,128]{3,2,1,0:T(8,128)}, u32[]{:S(2)}) copy-start(f32[5,4,128,128]{3,2,1,0:T(8,128)} %param.9) | copy-start | bytes 3932164
  50.7 30.0 %all-to-all-start = ((f32[32,1,2560]{2,1,0:T(1,128)}), f32[32,1,2560]{2,1,0:T(1,128)S(1)}, u32[]{:S(2)}, u32[]{:S(2)}) async-start(f32[32,1,2560]{2,1,0:T(1,128)} %reshape.183), calls=%async_computation | async-start | bytes 655360 | tf_op jit(solution)/shard_map/all_to_all | solution.py:84
  65.4 9.9 %collective-permute-start.2 = (f32[5,6,1,128]{3,0,2,1:T(8,128)S(1)}, f32[5,6,1,128]{3,0,2,1:T(8,128)S(1)}, u32[]{:S(2)}, u32[]{:S(2)}) collective-permute-start(f32[5,6,1,128]{3,0,2,1:T(8,128)S(1)} %get-tuple-element.7), channel_id=1, source_target_pairs={{0,1},{1,2},{2,3},{3,4},{4,5},{5,6},{6,7},{7,8},{8,9},{9,10},{10,1... | collective-permute-start | bytes 46088 | tf_op jit(solution)/shard_map/ppermute | solution.py:19
  65.8 9.6 %collective-permute-start.3 = (f32[5,6,1,128]{3,0,2,1:T(8,128)S(1)}, f32[5,6,1,128]{3,0,2,1:T(8,128)S(1)}, u32[]{:S(2)}, u32[]{:S(2)}) collective-permute-start(f32[5,6,1,128]{3,0,2,1:T(8,128)S(1)} %get-tuple-element.8), channel_id=1, source_target_pairs={{1,0},{2,1},{3,2},{4,3},{5,4},{6,5},{7,6},{8,7},{9,8},{10,9},{11,1... | collective-permute-start | bytes 46088 | tf_op jit(solution)/shard_map/ppermute | solution.py:22
  75.7 1.7 %copy-start.3 = (f32[5,6,130,128]{3,0,2,1:T(8,128)}, f32[5,6,130,128]{3,0,2,1:T(8,128)S(1)}, u32[]{:S(2)}) copy-start(f32[5,6,130,128]{3,0,2,1:T(8,128)S(1)} %maximum_multiply_fusion) | copy-start | bytes 5990404
  85.9 4.9 %copy-start.1 = (f32[5,4,128,127]{3,0,2,1:T(8,128)S(1)}, f32[5,4,128,127]{3,0,2,1:T(8,128)}, u32[]{:S(2)}) copy-start(f32[5,4,128,127]{3,0,2,1:T(8,128)} %copy.117) | copy-start | bytes 3901444
  86.0 4.9 %copy-start.2 = (f32[5,4,128,127]{3,0,2,1:T(8,128)S(1)}, f32[5,4,128,127]{3,0,2,1:T(8,128)}, u32[]{:S(2)}) copy-start(f32[5,4,128,127]{3,0,2,1:T(8,128)} %copy.116) | copy-start | bytes 3901444
  86.0 4.9 %copy-start.4 = (f32[5,6,130,128]{3,0,2,1:T(8,128)S(1)}, f32[5,6,130,128]{3,0,2,1:T(8,128)}, u32[]{:S(2)}) copy-start(f32[5,6,130,128]{3,0,2,1:T(8,128)} %copy-done.3) | copy-start | bytes 5990404
  86.0 4.9 %copy-start.5 = (f32[4,128,128]{2,1,0:T(8,128)S(1)}, f32[4,128,128]{2,1,0:T(8,128)}, u32[]{:S(2)}) copy-start(f32[4,128,128]{2,1,0:T(8,128)} %param.10) | copy-start | bytes 786436
  98.1 10.7 %collective-permute-start.4 = (f32[5,1,128,128]{3,0,2,1:T(8,128)S(1)}, f32[5,1,128,128]{3,0,2,1:T(8,128)S(1)}, u32[]{:S(2)}, u32[]{:S(2)}) collective-permute-start(f32[5,1,128,128]{3,0,2,1:T(8,128)S(1)} %get-tuple-element.9), channel_id=1, source_target_pairs={{0,32},{32,64},{64,96},{96,128},{128,160},{160,192},{192,224},{224... | collective-permute-start | bytes 983048 | tf_op jit(solution)/shard_map/ppermute | solution.py:19
  98.2 13.1 %collective-permute-start.5 = (f32[5,1,128,128]{3,0,2,1:T(8,128)S(1)}, f32[5,1,128,128]{3,0,2,1:T(8,128)S(1)}, u32[]{:S(2)}, u32[]{:S(2)}) collective-permute-start(f32[5,1,128,128]{3,0,2,1:T(8,128)S(1)} %get-tuple-element.10), channel_id=1, source_target_pairs={{32,0},{64,32},{96,64},{128,96},{160,128},{192,160},{224,192},{0,2... | collective-permute-start | bytes 983048 | tf_op jit(solution)/shard_map/ppermute | solution.py:22
  111.2 8.1 %collective-permute-start.6 = (f32[5,6,1,128]{3,0,2,1:T(8,128)S(1)}, f32[5,6,1,128]{3,0,2,1:T(8,128)S(1)}, u32[]{:S(2)}, u32[]{:S(2)}) collective-permute-start(f32[5,6,1,128]{3,0,2,1:T(8,128)S(1)} %get-tuple-element.5), channel_id=1, source_target_pairs={{0,1},{1,2},{2,3},{3,4},{4,5},{5,6},{6,7},{7,8},{8,9},{9,10},{10,1... | collective-permute-start | bytes 46088 | tf_op jit(solution)/shard_map/ppermute | solution.py:19
  111.3 8.0 %collective-permute-start.7 = (f32[5,6,1,128]{3,0,2,1:T(8,128)S(1)}, f32[5,6,1,128]{3,0,2,1:T(8,128)S(1)}, u32[]{:S(2)}, u32[]{:S(2)}) collective-permute-start(f32[5,6,1,128]{3,0,2,1:T(8,128)S(1)} %get-tuple-element.6), channel_id=1, source_target_pairs={{1,0},{2,1},{3,2},{4,3},{5,4},{6,5},{7,6},{8,7},{9,8},{10,9},{11,1... | collective-permute-start | bytes 46088 | tf_op jit(solution)/shard_map/ppermute | solution.py:22
where the time goes:
time: 128 us
  blocking collectives  36.6 us (29%)
  starting transfers between devices  26.4 us (21%)
  matrix products  26.1 us (20%)
  local copies, waits for them, and re-layouts  25.1 us (20%)
  waiting for transfers between devices  10.4 us (8%)
  other arithmetic  3.01 us (2%)
    all_gather x1, blocking collectives, body(): all_rows = lax.all_gather(rotor_face, 'circ', axis=1, tiled=True)  36.6 us
    dot_general x6, matrix products, contract(): jnp.einsum('fg,gtsa->ftsa', matrix, values, precision=lax.Precision.HIGHEST)  24.9 us
    ppermute x4, starting transfers between devices, with_halo(): lax.ppermute(lax.slice_in_dim(block, 0, width, axis=dim), axis, backward)  13.3 us
    unnamed x35, local copies, waits for them, and re-layouts  12.2 us
    all_to_all x1, starting transfers between devices, body(): received = lax.all_to_all(contributions, 'span', 0, 0, tiled=True)  11.2 us
    ppermute x4, waiting for transfers between devices, with_halo(): lax.ppermute(lax.slice_in_dim(block, block.shape[dim] - width, None, axis...  7.96 us
    gather x1, local copies, waits for them, and re-layouts, body(): rotated = jnp.take_along_axis(all_rows, source_rows[None], axis=1)  3.52 us
  transfers between devices with their start and end apart: 9, of which 2 were waited for; matrix products, arithmetic and copies ran while one was open for 19% of the time, Pallas kernels for 0%

commit v1 on v0

--- a/solution.py
+++ b/solution.py
@@ -65,7 +65,9 @@
     rows_local = rotor_face.shape[1]
     total_rows = rows_local * circ_count
     row_iota = jnp.arange(rows_local, dtype=jnp.int32)
-    all_rows = lax.all_gather(rotor_face, "circ", axis=1, tiled=True)
+    all_rows = jnp.concatenate(
+        lax.all_to_all(jnp.stack([rotor_face] * lax.axis_size("circ")), "circ", 0, 0), axis=1
+    )
     first_row = lax.axis_index("circ") * rows_local
     source_rows = (first_row + row_iota[:, None] - offsets[None, :]) % total_rows
     rotated = jnp.take_along_axis(all_rows, source_rows[None], axis=1)

time: 128 us -> 117 us (0.914)
  blocking collectives: 36.6 us -> 0 us
  waiting for transfers between devices: 10.4 us -> 22.3 us
  local copies, waits for them, and re-layouts: 25.1 us -> 32.8 us
  starting transfers between devices: 26.4 us -> 29.4 us
  other arithmetic: 3.01 us -> 5.79 us
    all_gather x1 -> x0, blocking collectives: 36.6 us -> none  [body(): all_rows = lax.all_gather(rotor_face, 'circ', axis=1, tiled=True)]
    all_to_all x1, waiting for transfers between devices: 0.01 us -> 8.53 us  [body(): received = lax.all_to_all(contributions, 'span', 0, 0, tiled=True)]
    all_to_all x0 -> x1, starting transfers between devices: none -> 5.79 us  [body(): lax.all_to_all(jnp.stack([rotor_face] * lax.axis_size('circ')), 'circ', 0...]
    all_to_all x1, starting transfers between devices: 11.2 us -> 6.26 us  [body(): received = lax.all_to_all(contributions, 'span', 0, 0, tiled=True)]
    ppermute x4, starting transfers between devices: 2 us -> 4.89 us  [with_halo(): lax.ppermute(lax.slice_in_dim(block, block.shape[dim] - width, None, axis...]
    unnamed x35 -> x34, local copies, waits for them, and re-layouts: 12.2 us -> 15 us
    gather x1, local copies, waits for them, and re-layouts: 3.52 us -> 5.93 us  [body(): rotated = jnp.take_along_axis(all_rows, source_rows[None], axis=1)]
    ppermute x4, waiting for transfers between devices: 2.43 us -> 4.32 us  [with_halo(): lax.ppermute(lax.slice_in_dim(block, 0, width, axis=dim), axis, backward)]
  transfers between devices with their start and end apart: 9 -> 10, of which waited for: 2 -> 3; matrix products, arithmetic and copies ran while one was open for 19% -> 28% of each run, Pallas kernels for 0% -> 0%
where the time goes in v1:
time: 117 us
  local copies, waits for them, and re-layouts  32.8 us (28%)
  starting transfers between devices  29.4 us (25%)
  matrix products  26.1 us (22%)
  waiting for transfers between devices  22.3 us (19%)
  other arithmetic  5.79 us (5%)
    dot_general x6, matrix products, contract(): jnp.einsum('fg,gtsa->ftsa', matrix, values, precision=lax.Precision.HIGHEST)  24.8 us
    unnamed x34, local copies, waits for them, and re-layouts  15 us
    ppermute x4, starting transfers between devices, with_halo(): lax.ppermute(lax.slice_in_dim(block, 0, width, axis=dim), axis, backward)  12.4 us
    ppermute x4, waiting for transfers between devices, with_halo(): lax.ppermute(lax.slice_in_dim(block, block.shape[dim] - width, None, axis...  9.48 us
    all_to_all x1, waiting for transfers between devices, body(): received = lax.all_to_all(contributions, 'span', 0, 0, tiled=True)  8.53 us
    all_to_all x1, starting transfers between devices, body(): received = lax.all_to_all(contributions, 'span', 0, 0, tiled=True)  6.26 us
    gather x1, local copies, waits for them, and re-layouts, body(): rotated = jnp.take_along_axis(all_rows, source_rows[None], axis=1)  5.93 us
    all_to_all x1, starting transfers between devices, body(): lax.all_to_all(jnp.stack([rotor_face] * lax.axis_size('circ')), 'circ', 0...  5.79 us
  transfers between devices with their start and end apart: 10, of which 3 were waited for; matrix products, arithmetic and copies ran while one was open for 28% of the time, Pallas kernels for 0%

profile of v1, /device:TPU:6, one launch (start us, length us, event | category | flops | bytes accessed | tf_op | source)
XLA Modules:
  0.0 116.8 jit_solution(2070466460169027169)
XLA Ops:
  0.0 1.5 %stack.2 = f32[8,5,4,128]{3,2,1,0:T(4,128)} broadcast(f32[5,4,128]{2,1,0:T(4,128)} %param.12), dimensions={1,2,3} | broadcast | bytes 92160 | tf_op jit(solution)/shard_map/stack | solution.py:69
  1.5 5.8 %all-to-all-start = ((f32[8,5,4,128]{3,2,1,0:T(4,128)}), f32[8,5,4,128]{3,2,1,0:T(4,128)S(1)}, u32[]{:S(2)}, u32[]{:S(2)}) async-start(f32[8,5,4,128]{3,2,1,0:T(4,128)} %stack.2), calls=%async_computation | async-start | bytes 163840 | tf_op jit(solution)/shard_map/all_to_all | solution.py:69
  7.3 1.1 fusion.49
  8.4 1.0 copy.116
  9.4 1.5 %collective-permute-start = (f32[5,1,128,128]{3,0,2,1:T(8,128)}, f32[5,1,128,128]{3,0,2,1:T(8,128)}, u32[]{:S(2)}, u32[]{:S(2)}) collective-permute-start(f32[5,1,128,128]{3,0,2,1:T(8,128)} %copy.116), channel_id=1, source_target_pairs={{0,32},{32,64},{64,96},{96,128},{128,160},{160,192},{192,224},{224... | collective-permute-start | bytes 983048 | tf_op jit(solution)/shard_map/ppermute | solution.py:19
  10.8 1.0 copy.117
  11.9 0.6 collective-permute-start.1
  12.4 0.1 compare_and_fusion
  12.5 0.1 fusion.41
  12.6 0.0 copy-start.7
  12.6 0.0 copy-start.8
  12.6 0.0 copy-start.9
  12.6 0.0 copy-start.10
  12.7 0.0 copy-start.11
  12.7 1.5 %fusion.50 = (f32[5,4,128,127]{3,2,1,0:T(8,128)}, f32[5,4,128,127]{3,2,1,0:T(8,128)S(1)}) fusion(f32[5,4,128,128]{3,2,1,0:T(8,128)S(1)} %copy-done), kind=kLoop, calls=%fused_computation.83 | loop fusion | bytes 5201920 | tf_op jit(solution)/shard_map/slice | solution.py:38
  14.2 0.2 select_reduce_fusion.1
  14.4 0.1 select_reduce_fusion
  14.5 0.1 dot_general.25
  14.6 0.1 copy.91
  14.7 3.5 %copy.115 = f32[5,4,128,127]{3,0,2,1:T(8,128)} copy(f32[5,4,128,127]{3,2,1,0:T(8,128)} %get-tuple-element.15) | data formatting | bytes 2600960
  18.2 2.2 %copy.114 = f32[5,4,128,127]{3,0,2,1:T(8,128)} copy(f32[5,4,128,127]{3,2,1,0:T(8,128)S(1)} %get-tuple-element.16) | data formatting | bytes 2600960
  20.4 0.0 all-to-all-done
  20.4 0.6 copy.75
  21.0 5.9 %gather_fusion = f32[512,5]{1,0:T(8,128)} fusion(f32[5,32,128]{0,2,1:T(8,128)S(1)} %bitcast.67, s32[512]{0:T(512)S(1)} %fusion.41), kind=kCustom, calls=%fused_computation | custom fusion | bytes 24576 | tf_op jit(solution)/shard_map/jit(take_along_axis)/gather | solution.py:73
  26.9 1.1 broadcast_select_fusion
  28.0 0.2 copy.95
  28.2 0.0 collective-permute-done
  28.2 1.1 constant_dynamic-update-slice_fusion.1
  29.3 0.8 copy_dynamic-update-slice_fusion
  30.1 1.1 constant_dynamic-update-slice_fusion
  31.2 0.1 collective-permute-start.2
  31.3 1.5 %copy-done.5 = f32[5,6,128,128]{3,0,2,1:T(8,128)} copy-done((f32[5,6,128,128]{3,0,2,1:T(8,128)}, f32[5,6,128,128]{3,0,2,1:T(8,128)S(1)}, u32[]{:S(2)}) %copy-start.5) | copy-done | bytes 1966104
  32.9 6.5 %collective-permute-start.3 = (f32[5,6,1,128]{3,0,2,1:T(8,128)S(1)}, f32[5,6,1,128]{3,0,2,1:T(8,128)S(1)}, u32[]{:S(2)}, u32[]{:S(2)}) collective-permute-start(f32[5,6,1,128]{3,0,2,1:T(8,128)S(1)} %get-tuple-element.8), channel_id=1, source_target_pairs={{1,0},{2,1},{3,2},{4,3},{5,4},{6,5},{7,6},{8,7},{9,8},{10,9},{11,1... | collective-permute-start | bytes 46088 | tf_op jit(solution)/shard_map/ppermute | solution.py:22
  39.4 1.2 %fusion.34 = f32[32,4,5,4,32]{4,0,3,2,1:T(8,128)S(1)} fusion(f32[32,4,4,1,1]{0,2,4,3,1:T(4,128)S(1)} %copy.91, f32[5,4,4,32]{3,2,1,0:T(4,128)S(1)} %copy.95), kind=kOutput, calls=%fused_computation.39 | convolution fusion | flops 3932160 | bytes 339968 | tf_op jit(solution)/shard_map/gk,ftkp->gftp/dot_general | solution.py:84
  40.6 0.8 copy.78
  41.5 1.6 %reshape.193 = f32[32,1,2560]{2,1,0:T(1,128)} reshape(f32[32,4,5,4,32]{4,3,2,1,0:T(4,128)S(1)} %copy.78) | data formatting | bytes 655360
  43.1 6.3 %all-to-all-start.1 = ((f32[32,1,2560]{2,1,0:T(1,128)}), f32[32,1,2560]{2,1,0:T(1,128)S(1)}, u32[]{:S(2)}, u32[]{:S(2)}) async-start(f32[32,1,2560]{2,1,0:T(1,128)} %reshape.193), calls=%async_computation.1 | async-start | bytes 655360 | tf_op jit(solution)/shard_map/all_to_all | solution.py:86
  49.3 0.0 collective-permute-done.2
  49.3 2.2 %maximum_multiply_fusion = f32[5,6,130,128]{3,0,2,1:T(8,128)S(1)} fusion(f32[5,6,1,128]{3,0,2,1:T(8,128)S(1)} %collective-permute-done.3, f32[5,6,128,128]{3,0,2,1:T(8,128)} %copy-done.5, f32[5,6,1,128]{3,0,2,1:T(8,128)S(1)} %collective-permute-done.2, f32[130]{0:T(256)S(1)} %not_convert_fusion), kind=kLoop, calls=%fused_computation.1 | loop fusion | flops 1497600 | bytes 3994120 | tf_op jit(solution)/shard_map/mul | solution.py:58
  51.6 1.6 %copy-done.3 = f32[5,6,130,128]{3,0,2,1:T(8,128)} copy-done((f32[5,6,130,128]{3,0,2,1:T(8,128)}, f32[5,6,130,128]{3,0,2,1:T(8,128)S(1)}, u32[]{:S(2)}) %copy-start.3) | copy-done | bytes 1996824
  53.2 3.4 %fusion.20 = f32[4,128,128,5]{2,3,1,0:T(8,128)} fusion(f32[5,6,130,128]{3,0,2,1:T(8,128)S(1)} %maximum_multiply_fusion, f32[1,5,5]{2,0,1:T(1,128)S(1)} %get-tuple-element.18), kind=kOutput, calls=%fused_computation.25 | convolution fusion | flops 19988480 | bytes 5507584 | tf_op jit(solution)/shard_map/fg,gtsa->ftsa/dot_general | solution.py:28
  56.6 8.5 %all-to-all-done.1 = f32[32,1,2560]{2,1,0:T(1,128)S(1)} async-done(((f32[32,1,2560]{2,1,0:T(1,128)}), f32[32,1,2560]{2,1,0:T(1,128)S(1)}, u32[]{:S(2)}, u32[]{:S(2)}) %all-to-all-start.1) | async-done | bytes 327712 | tf_op jit(solution)/shard_map/all_to_all | solution.py:86
  65.1 0.5 broadcast.285
  65.6 1.4 %reduce.1 = f32[32,2560]{1,0:T(8,128)S(1)} reduce(f32[32,1,2560]{2,1,0:T(1,128)S(1)} %all-to-all-done.1, f32[]{:T(128)} %broadcast.285), dimensions={1}, to_apply=%all_to_all.7.reduce_sub_computation | reduce | bytes 655364 | tf_op jit(solution)/shard_map/all_to_all | solution.py:86
  67.1 0.7 reshape.194
  67.7 0.3 reduce_sum.29
  68.0 0.9 copy.96
  68.9 1.4 %reshape.192 = f32[5,4,128,1]{3,0,2,1:T(8,128)S(1)} reshape(f32[5,4,4,32]{0,3,2,1:T(8,128)} %copy.96) | data formatting | bytes 20480 | tf_op jit(solution)/shard_map/broadcast_in_dim;reshape | solution.py:38
  70.3 0.0 copy-start.6
  70.4 4.9 %fusion.18 = f32[4,128,128,5]{2,3,1,0:T(8,128)S(1)} fusion(f32[5,4,128,127]{3,0,2,1:T(8,128)} %copy.114, f32[5,4,128,127]{3,0,2,1:T(8,128)} %copy.115, f32[5,4,128,1]{3,0,2,1:T(8,128)S(1)} %reshape.192, f32[1,5,5]{2,0,1:T(1,128)S(1)} %get-tuple-element.19), kind=kOutput, calls=%fused_computation.23 | convolution fusion | flops 20316160 | bytes 3922020 | tf_op jit(solution)/shard_map/fg,gtsa->ftsa/dot_general | solution.py:28
  75.3 7.1 %fusion.7 = f32[5,4,128,128]{3,0,2,1:T(8,128)S(1)} fusion(f32[4,128,128,5]{2,3,1,0:T(8,128)S(1)} %fusion.18, f32[4,128,128,5]{2,3,1,0:T(8,128)} %fusion.20, f32[5,6,130,128]{3,0,2,1:T(8,128)S(1)} %copy-done.4, f32[5,4,128,127]{3,0,2,1:T(8,128)S(1)} %copy-done.2, f32[4,128,128]{2,1,0:T(8,128)S(1)} %copy-done.6, f32[5,4,128,128]{3,2,1,0:T(8,128)S(1)} %copy-done, ...), kind=kOutput, calls=%fused_computation.14 | convolution fusion | flops 25559040 | bytes 25168384 | tf_op jit(solution)/shard_map/fg,gtsa->ftsa/dot_general | solution.py:28
  82.4 0.1 fusion.47
  82.4 3.0 %collective-permute-start.4 = (f32[5,1,128,128]{3,0,2,1:T(8,128)S(1)}, f32[5,1,128,128]{3,0,2,1:T(8,128)S(1)}, u32[]{:S(2)}, u32[]{:S(2)}) collective-permute-start(f32[5,1,128,128]{3,0,2,1:T(8,128)S(1)} %get-tuple-element.9), channel_id=1, source_target_pairs={{0,32},{32,64},{64,96},{96,128},{128,160},{160,192},{192,224},{224... | collective-permute-start | bytes 983048 | tf_op jit(solution)/shard_map/ppermute | solution.py:19
  85.5 0.7 fusion.48
  86.2 9.5 %collective-permute-done.4 = f32[5,1,128,128]{3,0,2,1:T(8,128)S(1)} collective-permute-done((f32[5,1,128,128]{3,0,2,1:T(8,128)S(1)}, f32[5,1,128,128]{3,0,2,1:T(8,128)S(1)}, u32[]{:S(2)}, u32[]{:S(2)}) %collective-permute-start.4) | collective-permute-done | bytes 327712 | tf_op jit(solution)/shard_map/ppermute | solution.py:19
  95.6 4.3 %collective-permute-done.5 = f32[5,1,128,128]{3,0,2,1:T(8,128)S(1)} collective-permute-done((f32[5,1,128,128]{3,0,2,1:T(8,128)S(1)}, f32[5,1,128,128]{3,0,2,1:T(8,128)S(1)}, u32[]{:S(2)}, u32[]{:S(2)}) %collective-permute-start.5) | collective-permute-done | bytes 327712 | tf_op jit(solution)/shard_map/ppermute | solution.py:22
  100.0 0.3 collective-permute-start.6
  100.3 5.3 %collective-permute-start.7 = (f32[5,6,1,128]{3,0,2,1:T(8,128)S(1)}, f32[5,6,1,128]{3,0,2,1:T(8,128)S(1)}, u32[]{:S(2)}, u32[]{:S(2)}) collective-permute-start(f32[5,6,1,128]{3,0,2,1:T(8,128)S(1)} %get-tuple-element.6), channel_id=1, source_target_pairs={{1,0},{2,1},{3,2},{4,3},{5,4},{6,5},{7,6},{8,7},{9,8},{10,9},{11,1... | collective-permute-start | bytes 46088 | tf_op jit(solution)/shard_map/ppermute | solution.py:22
  105.6 2.5 %fusion.8 = f32[4,128,128,5]{2,3,1,0:T(8,128)S(1)} fusion(f32[5,4,128,127]{3,0,2,1:T(8,128)S(1)} %get-tuple-element.12, f32[5,4,128,127]{3,0,2,1:T(8,128)S(1)} %get-tuple-element.11, f32[5,4,128,1]{3,0,2,1:T(8,128)S(1)} %reshape.192, f32[1,5,5]{2,0,1:T(1,128)S(1)} %get-tuple-element.19), kind=kOutput, calls=%fused_computation.15 | convolution fusion | flops 20316160 | bytes 3922020 | tf_op jit(solution)/shard_map/fg,gtsa->ftsa/dot_general | solution.py:28
  108.1 0.0 collective-permute-done.7
  108.1 0.4 maximum_multiply_fusion.1
  108.5 2.0 %fusion.10 = f32[4,128,128,5]{2,3,1,0:T(8,128)S(1)} fusion(f32[5,6,130,128]{3,0,2,1:T(8,128)S(1)} %maximum_multiply_fusion.1, f32[1,5,5]{2,0,1:T(1,128)S(1)} %get-tuple-element.18), kind=kOutput, calls=%fused_computation.17 | convolution fusion | flops 19988480 | bytes 5507584 | tf_op jit(solution)/shard_map/fg,gtsa->ftsa/dot_general | solution.py:28
  110.5 5.0 %fusion.3 = f32[5,4,128,128]{3,0,2,1:T(8,128)S(1)} fusion(f32[5,4,128,128]{3,0,2,1:T(8,128)S(1)} %fusion.7, f32[4,128,128,5]{2,3,1,0:T(8,128)S(1)} %fusion.8, f32[4,128,128,5]{2,3,1,0:T(8,128)S(1)} %fusion.10, f32[5,6,130,128]{3,0,2,1:T(8,128)S(1)} %maximum_multiply_fusion.1, f32[5,4,128,127]{3,0,2,1:T(8,128)S(1)} %get-tuple-element.12, ...), kind=kOutput, calls=%fused_computation.9 | convolution fusion | flops 25559040 | bytes 28051968 | tf_op jit(solution)/shard_map/fg,gtsa->ftsa/dot_general | solution.py:28
  115.5 1.3 %copy.88 = f32[5,4,128,128]{3,2,1,0:T(8,128)} copy(f32[5,4,128,128]{3,0,2,1:T(8,128)S(1)} %fusion.3) | data formatting | bytes 2621440 | tf_op jit(solution)/shard_map/sub | solution.py:46
  (28 shorter events, 0.1 us)
Async XLA Ops:
  0.0 12.6 %copy-start = (f32[5,4,128,128]{3,2,1,0:T(8,128)S(1)}, f32[5,4,128,128]{3,2,1,0:T(8,128)}, u32[]{:S(2)}) copy-start(f32[5,4,128,128]{3,2,1,0:T(8,128)} %param.9) | copy-start | bytes 3932164
  0.0 12.4 %copy-start.12 = (s32[128]{0:T(128)S(1)}, s32[128]{0:T(128)}, u32[]{:S(2)}) copy-start(s32[128]{0:T(128)} %param.13) | copy-start | bytes 1540
  1.5 18.9 %all-to-all-start = ((f32[8,5,4,128]{3,2,1,0:T(4,128)}), f32[8,5,4,128]{3,2,1,0:T(4,128)S(1)}, u32[]{:S(2)}, u32[]{:S(2)}) async-start(f32[8,5,4,128]{3,2,1,0:T(4,128)} %stack.2), calls=%async_computation | async-start | bytes 163840 | tf_op jit(solution)/shard_map/all_to_all | solution.py:69
  9.4 18.8 %collective-permute-start = (f32[5,1,128,128]{3,0,2,1:T(8,128)}, f32[5,1,128,128]{3,0,2,1:T(8,128)}, u32[]{:S(2)}, u32[]{:S(2)}) collective-permute-start(f32[5,1,128,128]{3,0,2,1:T(8,128)} %copy.116), channel_id=1, source_target_pairs={{0,32},{32,64},{64,96},{96,128},{128,160},{160,192},{192,224},{224... | collective-permute-start | bytes 983048 | tf_op jit(solution)/shard_map/ppermute | solution.py:19
  11.9 18.3 %collective-permute-start.1 = (f32[5,1,128,128]{3,0,2,1:T(8,128)}, f32[5,1,128,128]{3,0,2,1:T(8,128)}, u32[]{:S(2)}, u32[]{:S(2)}) collective-permute-start(f32[5,1,128,128]{3,0,2,1:T(8,128)} %copy.117), channel_id=1, source_target_pairs={{32,0},{64,32},{96,64},{128,96},{160,128},{192,160},{224,192},{0,2... | collective-permute-start | bytes 983048 | tf_op jit(solution)/shard_map/ppermute | solution.py:22
  12.6 1.6 %copy-start.7 = (f32[3,5,5]{2,0,1:T(4,128)S(1)}, f32[3,5,5]{2,0,1:T(4,128)}, u32[]{:S(2)}) copy-start(f32[3,5,5]{2,0,1:T(4,128)} %param.11) | copy-start | bytes 904
  12.6 1.6 %copy-start.8 = (s32[1,4,4]{2,1,0:T(4,128)S(1)}, s32[1,4,4]{2,1,0:T(4,128)}, u32[]{:S(2)}) copy-start(s32[1,4,4]{2,1,0:T(4,128)} %param.15) | copy-start | bytes 196
  12.6 1.6 %copy-start.9 = (s32[1,4,4]{2,1,0:T(4,128)S(1)}, s32[1,4,4]{2,1,0:T(4,128)}, u32[]{:S(2)}) copy-start(s32[1,4,4]{2,1,0:T(4,128)} %param.14) | copy-start | bytes 196
  12.6 1.6 %copy-start.10 = (s32[1,4,4]{2,1,0:T(4,128)S(1)}, s32[1,4,4]{2,1,0:T(4,128)}, u32[]{:S(2)}) copy-start(s32[1,4,4]{2,1,0:T(4,128)} %param.16) | copy-start | bytes 196
  12.7 1.6 %copy-start.11 = (f32[16]{0:T(128)S(1)}, f32[16]{0:T(128)}, u32[]{:S(2)}) copy-start(f32[16]{0:T(128)} %param.17) | copy-start | bytes 196
  31.2 1.7 %copy-start.5 = (f32[5,6,128,128]{3,0,2,1:T(8,128)}, f32[5,6,128,128]{3,0,2,1:T(8,128)S(1)}, u32[]{:S(2)}) copy-start(f32[5,6,128,128]{3,0,2,1:T(8,128)S(1)} %constant_dynamic-update-slice_fusion) | copy-start | bytes 5898244
  31.2 18.1 %collective-permute-start.2 = (f32[5,6,1,128]{3,0,2,1:T(8,128)S(1)}, f32[5,6,1,128]{3,0,2,1:T(8,128)S(1)}, u32[]{:S(2)}, u32[]{:S(2)}) collective-permute-start(f32[5,6,1,128]{3,0,2,1:T(8,128)S(1)} %get-tuple-element.7), channel_id=1, source_target_pairs={{0,1},{1,2},{2,3},{3,4},{4,5},{5,6},{6,7},{7,8},{8,9},{9,10},{10,1... | collective-permute-start | bytes 46088 | tf_op jit(solution)/shard_map/ppermute | solution.py:19
  32.9 16.5 %collective-permute-start.3 = (f32[5,6,1,128]{3,0,2,1:T(8,128)S(1)}, f32[5,6,1,128]{3,0,2,1:T(8,128)S(1)}, u32[]{:S(2)}, u32[]{:S(2)}) collective-permute-start(f32[5,6,1,128]{3,0,2,1:T(8,128)S(1)} %get-tuple-element.8), channel_id=1, source_target_pairs={{1,0},{2,1},{3,2},{4,3},{5,4},{6,5},{7,6},{8,7},{9,8},{10,9},{11,1... | collective-permute-start | bytes 46088 | tf_op jit(solution)/shard_map/ppermute | solution.py:22
  43.1 22.1 %all-to-all-start.1 = ((f32[32,1,2560]{2,1,0:T(1,128)}), f32[32,1,2560]{2,1,0:T(1,128)S(1)}, u32[]{:S(2)}, u32[]{:S(2)}) async-start(f32[32,1,2560]{2,1,0:T(1,128)} %reshape.193), calls=%async_computation.1 | async-start | bytes 655360 | tf_op jit(solution)/shard_map/all_to_all | solution.py:86
  51.6 1.7 %copy-start.3 = (f32[5,6,130,128]{3,0,2,1:T(8,128)}, f32[5,6,130,128]{3,0,2,1:T(8,128)S(1)}, u32[]{:S(2)}) copy-start(f32[5,6,130,128]{3,0,2,1:T(8,128)S(1)} %maximum_multiply_fusion) | copy-start | bytes 5990404
  70.3 4.9 %copy-start.1 = (f32[5,4,128,127]{3,0,2,1:T(8,128)S(1)}, f32[5,4,128,127]{3,0,2,1:T(8,128)}, u32[]{:S(2)}) copy-start(f32[5,4,128,127]{3,0,2,1:T(8,128)} %copy.115) | copy-start | bytes 3901444
  70.3 4.9 %copy-start.2 = (f32[5,4,128,127]{3,0,2,1:T(8,128)S(1)}, f32[5,4,128,127]{3,0,2,1:T(8,128)}, u32[]{:S(2)}) copy-start(f32[5,4,128,127]{3,0,2,1:T(8,128)} %copy.114) | copy-start | bytes 3901444
  70.3 4.9 %copy-start.4 = (f32[5,6,130,128]{3,0,2,1:T(8,128)S(1)}, f32[5,6,130,128]{3,0,2,1:T(8,128)}, u32[]{:S(2)}) copy-start(f32[5,6,130,128]{3,0,2,1:T(8,128)} %copy-done.3) | copy-start | bytes 5990404
  70.3 4.9 %copy-start.6 = (f32[4,128,128]{2,1,0:T(8,128)S(1)}, f32[4,128,128]{2,1,0:T(8,128)}, u32[]{:S(2)}) copy-start(f32[4,128,128]{2,1,0:T(8,128)} %param.10) | copy-start | bytes 786436
  82.4 13.2 %collective-permute-start.4 = (f32[5,1,128,128]{3,0,2,1:T(8,128)S(1)}, f32[5,1,128,128]{3,0,2,1:T(8,128)S(1)}, u32[]{:S(2)}, u32[]{:S(2)}) collective-permute-start(f32[5,1,128,128]{3,0,2,1:T(8,128)S(1)} %get-tuple-element.9), channel_id=1, source_target_pairs={{0,32},{32,64},{64,96},{96,128},{128,160},{160,192},{192,224},{224... | collective-permute-start | bytes 983048 | tf_op jit(solution)/shard_map/ppermute | solution.py:19
  85.5 14.5 %collective-permute-start.5 = (f32[5,1,128,128]{3,0,2,1:T(8,128)S(1)}, f32[5,1,128,128]{3,0,2,1:T(8,128)S(1)}, u32[]{:S(2)}, u32[]{:S(2)}) collective-permute-start(f32[5,1,128,128]{3,0,2,1:T(8,128)S(1)} %get-tuple-element.10), channel_id=1, source_target_pairs={{32,0},{64,32},{96,64},{128,96},{160,128},{192,160},{224,192},{0,2... | collective-permute-start | bytes 983048 | tf_op jit(solution)/shard_map/ppermute | solution.py:22
  100.0 8.1 %collective-permute-start.6 = (f32[5,6,1,128]{3,0,2,1:T(8,128)S(1)}, f32[5,6,1,128]{3,0,2,1:T(8,128)S(1)}, u32[]{:S(2)}, u32[]{:S(2)}) collective-permute-start(f32[5,6,1,128]{3,0,2,1:T(8,128)S(1)} %get-tuple-element.5), channel_id=1, source_target_pairs={{0,1},{1,2},{2,3},{3,4},{4,5},{5,6},{6,7},{7,8},{8,9},{9,10},{10,1... | collective-permute-start | bytes 46088 | tf_op jit(solution)/shard_map/ppermute | solution.py:19
  100.3 7.8 %collective-permute-start.7 = (f32[5,6,1,128]{3,0,2,1:T(8,128)S(1)}, f32[5,6,1,128]{3,0,2,1:T(8,128)S(1)}, u32[]{:S(2)}, u32[]{:S(2)}) collective-permute-start(f32[5,6,1,128]{3,0,2,1:T(8,128)S(1)} %get-tuple-element.6), channel_id=1, source_target_pairs={{1,0},{2,1},{3,2},{4,3},{5,4},{6,5},{7,6},{8,7},{9,8},{10,9},{11,1... | collective-permute-start | bytes 46088 | tf_op jit(solution)/shard_map/ppermute | solution.py:22
